TPU v7x, 32 devices: a whole 2x2x4 slice. The times are simulated.
32 devices in a mesh: groups: 2 (over y), rows: 16 (over z, x, core).
Axes of the slice: x: 2, y: 2, z: 4, core: 2. Of those that a mesh axis runs over, the one named last changes fastest.
Arguments:
- queries: bfloat16 [32, 4096], P(('groups', 'rows')), parts along dimension 0, may hold values from -135 to 135
- keys: bfloat16 [32, 384, 512], P(('groups', 'rows')), parts along dimension 0, may hold values from -4.5 to 4.5
- values: bfloat16 [32, 384, 512], P(('groups', 'rows')), parts along dimension 0, may hold values from -4.5 to 4.5
- lengths: int32 [32], P(('groups', 'rows')), parts along dimension 0, may hold values from 2 to 384
- resid: bfloat16 [32, 4096], P(('groups', 'rows')), parts along dimension 0, may hold values from -6 to 6
- out_weight: bfloat16 [4096, 4096], P('rows'), may hold values from -0.09375 to 0.09375
- chat_ids: int32 [256], replicated, may hold values from 0 to 8191, as said below
- enc_weight: bfloat16 [4096, 8192], P(None, 'rows'), may hold values from -0.09375 to 0.09375
- enc_bias: float32 [8192], P('rows'), may hold values from -3 to 3
- dec_weight: bfloat16 [8192, 4096], P('rows'), may hold values from -0.09375 to 0.09375
- dec_bias: float32 [4096], replicated, may hold values from -3 to 3
Outputs:
- spliced: bfloat16 [32, 4096], P(('groups', 'rows')), parts along dimension 0
- activity: bfloat16 [32, 8192], P('groups', 'rows'), parts along dimension 0
There are 2 independent parts, one for each index of `groups`. A program takes and returns all parts, laid end to end along the dimension named above; an argument that names none is the same for every part. Nothing has to cross between parts.
Inputs may be any that keep to these rules, and one draw needn't show every extreme that they name: `chat_ids`: 256 distinct latent numbers.
All inputs are finite; a program needn't handle non-finite values.
Results may differ from a plain program's by a relative error of at most 0.0057.
Values may be sent and summed in bfloat16 or wider, within the bound.
No kernel may reach another device: no remote copies, remote signals or barrier semaphores. Data moves between devices by JAX's collectives and lax.ppermute only.
A program may use at most 64 MiB of HBM per device.

v0:
```python
import jax
import jax.numpy as jnp
from jax import lax
from jax.sharding import PartitionSpec as P

HEAD_DIM = 128


def shards(
    queries,
    keys,
    values,
    lengths,
    resid,
    out_weight,
    chat_ids,
    enc_weight,
    enc_bias,
    dec_weight,
    dec_bias,
):
    rows_here = queries.shape[0]
    cache_span = keys.shape[1]
    key_width = keys.shape[2]
    kv_count = key_width // HEAD_DIM
    group_size = queries.shape[1] // key_width
    query_heads = queries.reshape(rows_here, kv_count, group_size, HEAD_DIM)
    key_heads = keys.reshape(rows_here, cache_span, kv_count, HEAD_DIM)
    value_heads = values.reshape(rows_here, cache_span, kv_count, HEAD_DIM)
    scores = jnp.einsum(
        "rkgd,rskd->rkgs", query_heads, key_heads, preferred_element_type=jnp.float32
    )
    scores = scores / jnp.sqrt(jnp.float32(HEAD_DIM))
    visible = lax.broadcasted_iota(jnp.int32, (rows_here, cache_span), 1) < lengths[:, None]
    scores = jnp.where(visible[:, None, None, :], scores, -jnp.inf)
    highest = jnp.max(scores, axis=-1, keepdims=True)
    expo = jnp.exp(scores - highest)
    weights = (expo / jnp.sum(expo, axis=-1, keepdims=True)).astype(jnp.bfloat16)
    attended = jnp.einsum(
        "rkgs,rskd->rkgd", weights, value_heads, preferred_element_type=jnp.float32
    )
    attended = attended.astype(jnp.bfloat16).reshape(rows_here, kv_count * group_size * HEAD_DIM)
    features = lax.all_to_all(attended, "rows", split_axis=1, concat_axis=0, tiled=True)
    partial_value = jnp.dot(features, out_weight, preferred_element_type=jnp.float32)
    lat_here = enc_weight.shape[1]
    latent_ids = lax.axis_index("rows") * lat_here + lax.broadcasted_iota(jnp.int32, (lat_here,), 0)
    listed = jnp.any(chat_ids[:, None] == latent_ids[None, :], axis=0)
    row_start = lax.axis_index("rows") * rows_here
    own_rows = lax.dynamic_slice_in_dim(partial_value, row_start, rows_here, 0) + resid.astype(
        jnp.float32
    )
    partial_value = lax.dynamic_update_slice_in_dim(partial_value, own_rows, row_start, 0)
    hidden = lax.psum(partial_value, "rows").astype(jnp.bfloat16)
    activity = jnp.where(
        listed[None, :],
        0.0,
        jax.nn.relu(
            jnp.dot(hidden, enc_weight, preferred_element_type=jnp.float32) + enc_bias[None, :]
        ),
    ).astype(jnp.bfloat16)
    rebuilt = lax.psum_scatter(
        jnp.dot(activity, dec_weight, preferred_element_type=jnp.float32),
        "rows",
        scatter_dimension=0,
        tiled=True,
    )
    spliced = (rebuilt + dec_bias[None, :]).astype(jnp.bfloat16)
    return (spliced, activity)


def solution(mesh):
    placed = (
        P(("groups", "rows"), None),
        P(("groups", "rows"), None, None),
        P(("groups", "rows"), None, None),
        P(("groups", "rows")),
        P(("groups", "rows"), None),
        P("rows", None),
        P(),
        P(None, "rows"),
        P("rows"),
        P("rows", None),
        P(),
    )
    return jax.shard_map(
        shards,
        mesh=mesh,
        in_specs=placed,
        out_specs=(P(("groups", "rows"), None), P("groups", "rows")),
        check_vma=False,
    )
```

profile of v0, /device:TPU:0, one launch (start us, length us, event | category | flops | bytes accessed | tf_op | source)
XLA Modules:
  0.0 189.1 jit_solution(12662302225228097001)
XLA Ops:
  7.2 0.0 copy-start
  7.2 1.2 reshape.68
  9.1 0.8 reduce.4
  9.9 0.2 fusion.3
  10.1 0.2 fusion.16
  10.3 1.1 reshape.69
  11.4 0.2 convolution_convert_fusion
  11.7 0.5 broadcast.26
  12.2 0.7 reduce.5
  12.9 0.6 reshape.72
  13.5 7.4 %all-to-all-start = ((bf16[16,2,128]{2,1,0:T(2,128)(2,1)}), bf16[16,2,128]{2,1,0:T(2,128)(2,1)S(1)}, u32[]{:S(2)}, u32[]{:S(2)}) async-start(bf16[16,2,128]{2,1,0:T(2,128)(2,1)} %reshape.72), calls=%async_computation | async-start | bytes 16384 | tf_op jit(solution)/shard_map/all_to_all | solution.py:43
  20.9 0.0 all-reduce.4.cloned.1.call-start
  20.9 0.8 compare_reduce_fusion
  21.8 5.5 %all-to-all-done = bf16[16,2,128]{2,1,0:T(2,128)(2,1)S(1)} async-done(((bf16[16,2,128]{2,1,0:T(2,128)(2,1)}), bf16[16,2,128]{2,1,0:T(2,128)(2,1)S(1)}, u32[]{:S(2)}, u32[]{:S(2)}) %all-to-all-start) | async-done | bytes 8224 | tf_op jit(solution)/shard_map/all_to_all | solution.py:43
  27.3 0.4 fusion.13
  27.7 0.4 dynamic_update_slice.3
  28.1 59.8 %all-reduce.5 = bf16[16,4096]{1,0:T(8,128)(2,1)S(1)} all-reduce(f32[16,4096]{1,0:T(8,128)S(1)} %dynamic_update_slice.3), channel_id=1, replica_groups=mesh['groups'=2,'rows'=16] {'rows'}, use_global_device_ids=true, to_apply=%region_3.4 | all-reduce | flops 65536 | bytes 393216 | tf_op jit(solution)/shard_map/psum | solution.py:53
  88.0 3.0 %fusion.6 = bf16[16,512]{1,0:T(8,128)(2,1)S(1)} fusion(bf16[4096,512]{1,0:T(8,128)(2,1)} %param.18, bf16[16,4096]{1,0:T(8,128)(2,1)S(1)} %all-reduce.5, f32[512]{0:T(512)S(1)} %copy-done.5, pred[512]{0:T(512)(128)(4,1)S(1)} %compare_reduce_fusion), kind=kOutput, calls=%fused_computation.8 | convolution fusion | flops 67141632 | bytes 4344320 | tf_op jit(solution)/shard_map/dot_general | solution.py:58
  91.0 0.4 copy-done.1
  91.4 1.4 fusion.17
  92.7 0.0 all-reduce.4.cloned.1.call-update
  92.8 0.7 dynamic-slice
  93.4 86.5 %all-reduce.4.cloned.1.call-done = f32[16,4096]{1,0:T(8,128)} async-done(((f32[16,4096]{1,0:T(8,128)}), f32[16,4096]{1,0:T(8,128)}) %all-reduce.4.cloned.1.call-update) | async-done | bytes 262160
  180.0 2.2 %fusion.11 = bf16[1,4096]{1,0:T(2,128)(2,1)} fusion(f32[1,4096]{1,0:T(1,128)S(1)} %bitcast.21, f32[16,4096]{1,0:T(8,128)} %all-reduce.4.cloned.1.call-done, u32[]{:T(128)} %bitcast.2), kind=kLoop, calls=%fused_computation.17 | loop fusion | flops 8192 | bytes 40964 | tf_op jit(solution)/shard_map/convert_element_type | solution.py:67
  (17 shorter events, 0.1 us)
Async XLA Ops:
  7.2 20.1 %copy-start = (bf16[256,4096]{1,0:T(8,128)(2,1)S(1)}, bf16[256,4096]{1,0:T(8,128)(2,1)}, u32[]{:S(2)}) copy-start(bf16[256,4096]{1,0:T(8,128)(2,1)} %param.16) | copy-start | bytes 6291460
  7.2 20.5 %copy-start.3 = (bf16[1,4096]{1,0:T(2,128)(2,1)S(1)}, bf16[1,4096]{1,0:T(2,128)(2,1)}, u32[]{:S(2)}) copy-start(bf16[1,4096]{1,0:T(2,128)(2,1)} %param.15) | copy-start | bytes 24580
  7.2 80.7 %copy-start.5 = (f32[512]{0:T(512)S(1)}, f32[512]{0:T(512)}, u32[]{:S(2)}) copy-start(f32[512]{0:T(512)} %param.19) | copy-start | bytes 6148
  13.5 13.8 %all-to-all-start = ((bf16[16,2,128]{2,1,0:T(2,128)(2,1)}), bf16[16,2,128]{2,1,0:T(2,128)(2,1)S(1)}, u32[]{:S(2)}, u32[]{:S(2)}) async-start(bf16[16,2,128]{2,1,0:T(2,128)(2,1)} %reshape.72), calls=%async_computation | async-start | bytes 16384 | tf_op jit(solution)/shard_map/all_to_all | solution.py:43
  20.9 159.1 %all-reduce.4.cloned.1.call-start = ((), (), s32[]{:S(2)}) async-start(), calls=%async_computation.1 | async-start | bytes 524288
  87.9 3.5 %copy-start.1 = (bf16[512,4096]{1,0:T(8,128)(2,1)S(1)}, bf16[512,4096]{1,0:T(8,128)(2,1)}, u32[]{:S(2)}) copy-start(bf16[512,4096]{1,0:T(8,128)(2,1)} %param.20) | copy-start | bytes 12582916
  87.9 4.8 %copy-start.6 = (u32[32]{0:T(128)S(1)}, u32[32]{0:T(128)}, u32[]{:S(2)}) copy-start(u32[32]{0:T(128)} %constant.28) | copy-start | bytes 388
  88.0 92.0 %copy-start.4 = (f32[4096]{0:T(1024)S(1)}, f32[4096]{0:T(1024)}, u32[]{:S(2)}) copy-start(f32[4096]{0:T(1024)} %param.21) | copy-start | bytes 49156
  91.4 90.8 %copy-start.2 = (bf16[16,512]{1,0:T(8,128)(2,1)}, bf16[16,512]{1,0:T(8,128)(2,1)S(1)}, u32[]{:S(2)}) copy-start(bf16[16,512]{1,0:T(8,128)(2,1)S(1)} %fusion.6) | copy-start | bytes 49156
Sparse Core Ops, SparseCore 0:
  92.9 87.0 all-reduce.3
where the time goes:
time: 189 us
  waiting for transfers between devices  92 us (49%)
  blocking collectives  59.8 us (32%)
  between operations  14.8 us (8%)
  starting transfers between devices  7.43 us (4%)
  matrix products  5.2 us (3%)
  local copies, waits for them, and re-layouts  5.01 us (3%)
  other arithmetic  4.74 us (3%)
    unnamed x2, waiting for transfers between devices  86.6 us
    psum x1, blocking collectives, shards(): hidden = lax.psum(partial_value, 'rows').astype(jnp.bfloat16)  59.8 us
    all_to_all x1, starting transfers between devices, shards(): lax.all_to_all(attended, 'rows', split_axis=1, concat_axis=0, tiled=True)  7.39 us
    all_to_all x1, waiting for transfers between devices, shards(): lax.all_to_all(attended, 'rows', split_axis=1, concat_axis=0, tiled=True)  5.46 us
  transfers between devices with their start and end apart: 2, of which 2 were waited for; matrix products, arithmetic and copies ran while one was open for 1% of the time, Pallas kernels for 0%

commit v1 on v0

--- a/solution.py
+++ b/solution.py
@@ -1,9 +1,17 @@
+import functools
 import jax
 import jax.numpy as jnp
 from jax import lax
 from jax.sharding import PartitionSpec as P
 
 HEAD_DIM = 128
+
+
+def edit_sectors_on_mesh(a0, which_axis):
+    return lax.all_gather(a0, axis_name=which_axis).sum(axis=0)
+
+
+array_search = functools.partial(edit_sectors_on_mesh, which_axis="rows")
 
 
 def shards(
@@ -50,7 +58,7 @@
         jnp.float32
     )
     partial_value = lax.dynamic_update_slice_in_dim(partial_value, own_rows, row_start, 0)
-    hidden = lax.psum(partial_value, "rows").astype(jnp.bfloat16)
+    hidden = array_search(partial_value).astype(jnp.bfloat16)
     activity = jnp.where(
         listed[None, :],
         0.0,

time: 189 us -> 182 us (0.963)
  blocking collectives: 59.8 us -> 0 us
  waiting for transfers between devices: 92 us -> 142 us
    psum x1 -> x0, blocking collectives: 59.8 us -> none  [shards(): hidden = lax.psum(partial_value, 'rows').astype(jnp.bfloat16)]
    all_gather x0 -> x1, waiting for transfers between devices: none -> 47.6 us  [edit_sectors_on_mesh(): return lax.all_gather(a0, axis_name=which_axis).sum(axis=0)]
    reduce_sum x0 -> x1, other arithmetic: none -> 2.39 us  [edit_sectors_on_mesh(): return lax.all_gather(a0, axis_name=which_axis).sum(axis=0)]
    unnamed x2 -> x3, waiting for transfers between devices: 86.6 us -> 87.8 us
  transfers between devices with their start and end apart: 2 -> 3, of which waited for: 2 -> 3; matrix products, arithmetic and copies ran while one was open for 1% -> 0% of each run, Pallas kernels for 0% -> 0%
where the time goes in v1:
time: 182 us; the launch traced here: 181 us
  waiting for transfers between devices  142 us (78%)
  between operations  14.9 us (8%)
  starting transfers between devices  7.47 us (4%)
  other arithmetic  6.46 us (4%)
  local copies, waits for them, and re-layouts  5.71 us (3%)
  matrix products  5.2 us (3%)
    unnamed x3, waiting for transfers between devices  87.8 us
    all_gather x1, waiting for transfers between devices, edit_sectors_on_mesh(): return lax.all_gather(a0, axis_name=which_axis).sum(axis=0)  47.6 us
    all_to_all x1, starting transfers between devices, shards(): lax.all_to_all(attended, 'rows', split_axis=1, concat_axis=0, tiled=True)  7.39 us
    all_to_all x1, waiting for transfers between devices, shards(): lax.all_to_all(attended, 'rows', split_axis=1, concat_axis=0, tiled=True)  6.31 us
  transfers between devices with their start and end apart: 3, of which 3 were waited for; matrix products, arithmetic and copies ran while one was open for 0% of the time, Pallas kernels for 0%

profile of v1, /device:TPU:0, one launch (start us, length us, event | category | flops | bytes accessed | tf_op | source)
XLA Modules:
  0.0 181.4 jit_solution(2504364416962517659)
XLA Ops:
  7.2 1.2 reshape.70
  9.1 0.8 reduce.4
  9.9 0.2 fusion.3
  10.1 0.2 fusion.16
  10.3 1.1 reshape.71
  11.4 0.2 convolution_convert_fusion
  11.7 0.5 broadcast.26
  12.2 0.7 reduce.5
  12.9 0.6 reshape.74
  13.5 7.4 %all-to-all-start = ((bf16[16,2,128]{2,1,0:T(2,128)(2,1)}), bf16[16,2,128]{2,1,0:T(2,128)(2,1)S(1)}, u32[]{:S(2)}, u32[]{:S(2)}) async-start(bf16[16,2,128]{2,1,0:T(2,128)(2,1)} %reshape.74), calls=%async_computation | async-start | bytes 16384 | tf_op jit(solution)/shard_map/all_to_all | solution.py:51
  21.0 6.3 %all-to-all-done = bf16[16,2,128]{2,1,0:T(2,128)(2,1)S(1)} async-done(((bf16[16,2,128]{2,1,0:T(2,128)(2,1)}), bf16[16,2,128]{2,1,0:T(2,128)(2,1)S(1)}, u32[]{:S(2)}, u32[]{:S(2)}) %all-to-all-start) | async-done | bytes 8224 | tf_op jit(solution)/shard_map/all_to_all | solution.py:51
  27.3 0.4 fusion.13
  27.7 0.4 dynamic_update_slice.4
  28.1 0.7 copy-done.2
  28.8 0.0 all-reduce.3.cloned.1.call-start
  28.9 0.2 compare_reduce_fusion
  29.0 47.6 %all-gather.2.cloned.1.call-done = f32[16,16,4096]{2,1,0:T(8,128)} async-done(((f32[1,16,4096]{2,1,0:T(8,128)}), f32[16,16,4096]{2,1,0:T(8,128)}) %all-gather.2.cloned.1.call-update) | async-done | bytes 4194320 | tf_op jit(solution)/shard_map/all_gather | solution.py:11
  76.6 2.4 %reduce_sum.19 = bf16[16,4096]{1,0:T(8,128)(2,1)S(1)} reduce(f32[16,16,4096]{2,1,0:T(8,128)} %all-gather.2.cloned.1.call-done, f32[]{:T(128)} %constant.5.clone.1), dimensions={0}, to_apply=%region_3.4 | reduce | flops 983040 | bytes 4325380 | tf_op jit(solution)/shard_map/reduce_sum | solution.py:11
  79.1 3.0 %fusion.6 = bf16[16,512]{1,0:T(8,128)(2,1)S(1)} fusion(bf16[4096,512]{1,0:T(8,128)(2,1)} %param.18, bf16[16,4096]{1,0:T(8,128)(2,1)S(1)} %reduce_sum.19, f32[512]{0:T(512)S(1)} %copy-done.6, pred[512]{0:T(512)(128)(4,1)S(1)} %compare_reduce_fusion), kind=kOutput, calls=%fused_computation.8 | convolution fusion | flops 67141632 | bytes 4344320 | tf_op jit(solution)/shard_map/dot_general | solution.py:66
  82.1 0.4 copy-done.1
  82.5 1.4 fusion.17
  83.9 0.7 dynamic-slice
  84.6 87.8 %all-reduce.3.cloned.1.call-done = f32[16,4096]{1,0:T(8,128)} async-done(((f32[16,4096]{1,0:T(8,128)}), f32[16,4096]{1,0:T(8,128)}) %all-reduce.3.cloned.1.call-update) | async-done | bytes 262160
  172.3 2.2 %fusion.11 = bf16[1,4096]{1,0:T(2,128)(2,1)} fusion(f32[1,4096]{1,0:T(1,128)S(1)} %bitcast.25, f32[16,4096]{1,0:T(8,128)} %all-reduce.3.cloned.1.call-done, u32[]{:T(128)} %bitcast.4), kind=kLoop, calls=%fused_computation.17 | loop fusion | flops 8192 | bytes 40964 | tf_op jit(solution)/shard_map/convert_element_type | solution.py:75
  (24 shorter events, 0.2 us)
Async XLA Ops:
  7.2 20.1 %copy-start = (bf16[256,4096]{1,0:T(8,128)(2,1)S(1)}, bf16[256,4096]{1,0:T(8,128)(2,1)}, u32[]{:S(2)}) copy-start(bf16[256,4096]{1,0:T(8,128)(2,1)} %param.16) | copy-start | bytes 6291460
  7.2 20.5 %copy-start.4 = (bf16[1,4096]{1,0:T(2,128)(2,1)S(1)}, bf16[1,4096]{1,0:T(2,128)(2,1)}, u32[]{:S(2)}) copy-start(bf16[1,4096]{1,0:T(2,128)(2,1)} %param.15) | copy-start | bytes 24580
  7.2 21.7 %copy-start.7 = (s32[256]{0:T(256)S(1)}, s32[256]{0:T(256)}, u32[]{:S(2)}) copy-start(s32[256]{0:T(256)} %param.17) | copy-start | bytes 3076
  10.3 68.7 %copy-start.6 = (f32[512]{0:T(512)S(1)}, f32[512]{0:T(512)}, u32[]{:S(2)}) copy-start(f32[512]{0:T(512)} %param.19) | copy-start | bytes 6148
  13.5 13.8 %all-to-all-start = ((bf16[16,2,128]{2,1,0:T(2,128)(2,1)}), bf16[16,2,128]{2,1,0:T(2,128)(2,1)S(1)}, u32[]{:S(2)}, u32[]{:S(2)}) async-start(bf16[16,2,128]{2,1,0:T(2,128)(2,1)} %reshape.74), calls=%async_computation | async-start | bytes 16384 | tf_op jit(solution)/shard_map/all_to_all | solution.py:51
  20.9 55.7 %all-gather.2.cloned.1.call-start = ((), (), s32[]{:S(2)}) async-start(), calls=%async_computation.1 | async-start | bytes 4456448 | tf_op jit(solution)/shard_map/all_gather | solution.py:11
  28.1 0.7 copy-start.2
  28.8 143.5 %all-reduce.3.cloned.1.call-start = ((), (), s32[]{:S(2)}) async-start(), calls=%async_computation.2 | async-start | bytes 524288
  79.0 3.5 %copy-start.1 = (bf16[512,4096]{1,0:T(8,128)(2,1)S(1)}, bf16[512,4096]{1,0:T(8,128)(2,1)}, u32[]{:S(2)}) copy-start(bf16[512,4096]{1,0:T(8,128)(2,1)} %param.20) | copy-start | bytes 12582916
  79.0 4.8 %copy-start.8 = (u32[32]{0:T(128)S(1)}, u32[32]{0:T(128)}, u32[]{:S(2)}) copy-start(u32[32]{0:T(128)} %constant.29) | copy-start | bytes 388
  79.1 93.3 %copy-start.5 = (f32[4096]{0:T(1024)S(1)}, f32[4096]{0:T(1024)}, u32[]{:S(2)}) copy-start(f32[4096]{0:T(1024)} %param.21) | copy-start | bytes 49156
  82.5 92.1 %copy-start.3 = (bf16[16,512]{1,0:T(8,128)(2,1)}, bf16[16,512]{1,0:T(8,128)(2,1)S(1)}, u32[]{:S(2)}) copy-start(bf16[16,512]{1,0:T(8,128)(2,1)S(1)} %fusion.6) | copy-start | bytes 49156
Sparse Core Ops, SparseCore 0:
  28.9 47.6 all-gather.1
  84.0 88.3 all-reduce.2
